TPU v7x, 32 devices: a whole 2x2x4 slice. The times are simulated.
32 devices in a mesh: rec: 2 (over core), space: 16 (over z, y, x).
Axes of the slice: x: 2, y: 2, z: 4, core: 2. Of those that a mesh axis runs over, the one named last changes fastest.
Arguments:
- footprints: bfloat16 [32, 120, 8400], P(('rec', 'space')), may hold values from 0 to 1
- time_cov: bfloat16 [120, 120], replicated, may hold values from -1 to 3
- lat_cov: bfloat16 [70, 70], replicated, may hold values from -1 to 3
- lon_cov: bfloat16 [120, 120], replicated, may hold values from -1 to 3
Outputs:
- gram: float32 [32, 32], P(('rec', 'space'))
All inputs are finite; a program needn't handle non-finite values.
Results may differ from a plain program's by a relative error of at most 0.0003.
Values may be sent and summed in bfloat16 or wider, within the bound.
No kernel may reach another device: no remote copies, remote signals or barrier semaphores. Data moves between devices by JAX's collectives and lax.ppermute only.
A program may use at most 64 MiB of HBM per device.

v0:
```python
import jax
import jax.numpy as jnp
from jax import lax
from jax.sharding import PartitionSpec as P


def weigh_footprints(footprints, time_cov, lat_cov, lon_cov):
    receptors_here, time_count, cell_count = footprints.shape
    lat_count = lat_cov.shape[0]
    lon_count = lon_cov.shape[0]
    along_lon = jnp.dot(
        footprints.reshape(receptors_here * time_count * lat_count, lon_count),
        lon_cov,
        preferred_element_type=jnp.float32,
    ).astype(jnp.bfloat16)
    along_lat = jnp.einsum(
        "rab,ac->rcb",
        along_lon.reshape(receptors_here * time_count, lat_count, lon_count),
        lat_cov,
        preferred_element_type=jnp.float32,
    ).astype(jnp.bfloat16)
    return jnp.einsum(
        "rtc,ts->rsc",
        along_lat.reshape(receptors_here, time_count, cell_count),
        time_cov,
        preferred_element_type=jnp.float32,
    ).astype(jnp.bfloat16)


def flatten_padded(values, devices):
    receptors_here = values.shape[0]
    flat = values.reshape(receptors_here, -1)
    length = flat.shape[1]
    per_device = -(-length // devices)
    per_device = -(-per_device // 128) * 128
    return jnp.pad(flat, ((0, 0), (0, per_device * devices - length)))


def regroup(values):
    moved = (
        lax.all_to_all(
            lax.all_to_all(values[0], "space", split_axis=1, concat_axis=0, tiled=True),
            "rec",
            split_axis=1,
            concat_axis=0,
            tiled=True,
        ),
        lax.all_to_all(
            lax.all_to_all(values[1], "space", split_axis=1, concat_axis=0, tiled=True),
            "rec",
            split_axis=1,
            concat_axis=0,
            tiled=True,
        ),
    )
    return moved


def local(footprints, time_cov, lat_cov, lon_cov):
    rec_count = lax.axis_size("rec")
    space_count = lax.axis_size("space")
    devices = rec_count * space_count
    plain = flatten_padded(footprints, devices)
    weighted = flatten_padded(weigh_footprints(footprints, time_cov, lat_cov, lon_cov), devices)
    weighted_all, plain_all = regroup((weighted, plain))
    partial_value = lax.dot_general(
        weighted_all, plain_all, (((1,), (1,)), ((), ())), preferred_element_type=jnp.float32
    )
    return lax.psum_scatter(partial_value, ("rec", "space"), scatter_dimension=0, tiled=True)


def solution(mesh):
    in_specs = (P(("rec", "space"), None, None), P(), P(), P())
    out_specs = P(("rec", "space"), None)
    return jax.shard_map(local, mesh=mesh, in_specs=in_specs, out_specs=out_specs, check_vma=False)
```

profile of v0, /device:TPU:0, one launch (start us, length us, event | category | flops | bytes accessed | tf_op | source)
XLA Modules:
  0.0 254.2 jit_solution(8349191223248169489)
XLA Ops:
  0.0 5.8 %reshape.41 = bf16[8400,120]{1,0:T(8,128)(2,1)S(1)} reshape(bf16[1,120,8400]{2,1,0:T(8,128)(2,1)} %param.4) | data formatting | bytes 4032000 | tf_op jit(solution)/shard_map/reshape | solution.py:12
  7.9 4.1 %copy.15 = bf16[8400,120]{1,0:T(8,128)(2,1)} copy(bf16[8400,120]{0,1:T(8,128)(2,1)} %convolution_convert_fusion.1) | data formatting | bytes 4032000 | tf_op jit(solution)/shard_map/convert_element_type | solution.py:15
  12.0 2.8 %reshape.42 = bf16[120,70,120]{2,1,0:T(8,128)(2,1)S(1)} reshape(bf16[8400,120]{1,0:T(8,128)(2,1)} %copy.15) | data formatting | bytes 4032000 | tf_op jit(solution)/shard_map/reshape | solution.py:18
  14.8 2.2 convert_bitcast_fusion
  17.0 3.6 %copy.17 = bf16[120,70,120]{0,2,1:T(8,128)(2,1)S(1)} copy(bf16[120,70,120]{2,1,0:T(8,128)(2,1)} %convert_bitcast_fusion) | data formatting | bytes 4032000 | tf_op jit(solution)/shard_map/convert_element_type | solution.py:21
  22.7 4.7 %reshape.49 = bf16[1008000]{0:T(1024)(128)(2,1)S(1)} reshape(bf16[120,8400]{1,0:T(8,128)(2,1)} %fusion) | data formatting | bytes 4032000
  27.4 23.2 %reshape.44 = bf16[1,1008000]{1,0:T(2,128)(2,1)S(1)} reshape(bf16[1008000]{0:T(1024)(128)(2,1)S(1)} %reshape.49) | data formatting | bytes 4032000 | tf_op jit(solution)/shard_map/reshape | solution.py:32
  50.6 5.9 %pad.7 = bf16[1,1011712]{1,0:T(2,128)(2,1)} pad(bf16[1,1008000]{1,0:T(2,128)(2,1)S(1)} %reshape.44, bf16[]{:T(256)} %constant.2.clone.1), padding=0_0x0_3712 | pad | bytes 4039426 | tf_op jit(solution)/shard_map/jit(_pad)/pad | solution.py:36
  57.0 12.8 %reduce.4 = bf16[16,63232]{1,0:T(8,128)(2,1)S(1)} reduce(bf16[16,1,63232]{2,1,0:T(2,128)(2,1)} %bitcast.37, bf16[]{:T(256)} %broadcast.6), dimensions={1}, to_apply=%bitcast.22.reduce_sub_computation | reduce | bytes 4046850
  71.4 8.5 %all-to-all-start = ((bf16[16,2,31616]{2,1,0:T(2,128)(2,1)}), bf16[16,2,31616]{2,1,0:T(2,128)(2,1)}, u32[]{:S(2)}, u32[]{:S(2)}) async-start(bf16[16,2,31616]{2,1,0:T(2,128)(2,1)} %reshape.53), calls=%async_computation | async-start | bytes 4046848 | tf_op jit(solution)/shard_map/all_to_all | solution.py:42
  79.9 5.0 %reshape.51 = bf16[1008000]{0:T(1024)(128)(2,1)} reshape(bf16[1,120,8400]{2,1,0:T(8,128)(2,1)S(1)} %copy-done.2) | data formatting | bytes 4032000
  84.9 20.0 %reshape.45 = bf16[1,1008000]{1,0:T(2,128)(2,1)S(1)} reshape(bf16[1008000]{0:T(1024)(128)(2,1)} %reshape.51) | data formatting | bytes 4032000 | tf_op jit(solution)/shard_map/reshape | solution.py:32
  104.8 5.9 %pad.8 = bf16[1,1011712]{1,0:T(2,128)(2,1)} pad(bf16[1,1008000]{1,0:T(2,128)(2,1)S(1)} %reshape.45, bf16[]{:T(256)} %constant.2.clone.1), padding=0_0x0_3712 | pad | bytes 4039426 | tf_op jit(solution)/shard_map/jit(_pad)/pad | solution.py:36
  110.7 12.8 %reduce.5 = bf16[16,63232]{1,0:T(8,128)(2,1)S(1)} reduce(bf16[16,1,63232]{2,1,0:T(2,128)(2,1)} %bitcast.38, bf16[]{:T(256)} %broadcast.6), dimensions={1}, to_apply=%bitcast.24.reduce_sub_computation | reduce | bytes 4046850
  125.2 6.8 %all-to-all-start.2 = ((bf16[16,2,31616]{2,1,0:T(2,128)(2,1)}), bf16[16,2,31616]{2,1,0:T(2,128)(2,1)S(1)}, u32[]{:S(2)}, u32[]{:S(2)}) async-start(bf16[16,2,31616]{2,1,0:T(2,128)(2,1)} %reshape.55), calls=%async_computation.2 | async-start | bytes 4046848 | tf_op jit(solution)/shard_map/all_to_all | solution.py:49
  132.0 12.4 %reshape.54 = bf16[16,1,63232]{2,1,0:T(2,128)(2,1)} reshape(bf16[16,2,31616]{2,1,0:T(2,128)(2,1)} %all-to-all-done) | data formatting | bytes 4046848
  144.4 13.2 %bitcast_reduce_fusion.1 = bf16[16,63232]{1,0:T(8,128)(2,1)S(1)} fusion(bf16[16,1,63232]{2,1,0:T(2,128)(2,1)} %reshape.54), kind=kLoop, calls=%fused_computation.9 | loop fusion | bytes 4046848 | tf_op jit(solution)/shard_map/all_to_all | solution.py:42
  159.0 14.5 %all-to-all-done.2 = bf16[16,2,31616]{2,1,0:T(2,128)(2,1)S(1)} async-done(((bf16[16,2,31616]{2,1,0:T(2,128)(2,1)}), bf16[16,2,31616]{2,1,0:T(2,128)(2,1)S(1)}, u32[]{:S(2)}, u32[]{:S(2)}) %all-to-all-start.2) | async-done | bytes 2023456 | tf_op jit(solution)/shard_map/all_to_all | solution.py:49
  173.6 5.0 %all-to-all-start.1 = ((bf16[16,2,31616]{2,0,1:T(8,128)(2,1)}), bf16[16,2,31616]{2,0,1:T(8,128)(2,1)}, u32[]{:S(2)}, u32[]{:S(2)}) async-start(bf16[16,2,31616]{2,0,1:T(8,128)(2,1)} %bitcast.42), calls=%async_computation.1 | async-start | bytes 4046848 | tf_op jit(solution)/shard_map/all_to_all | solution.py:41
  178.6 9.0 %reshape.56 = bf16[16,1,63232]{2,1,0:T(2,128)(2,1)} reshape(bf16[16,2,31616]{2,1,0:T(2,128)(2,1)S(1)} %all-to-all-done.2) | data formatting | bytes 4046848
  187.6 13.2 %bitcast_reduce_fusion = bf16[16,63232]{1,0:T(8,128)(2,1)S(1)} fusion(bf16[16,1,63232]{2,1,0:T(2,128)(2,1)} %reshape.56), kind=kLoop, calls=%fused_computation.8 | loop fusion | bytes 4046848 | tf_op jit(solution)/shard_map/all_to_all | solution.py:49
  200.9 5.4 %all_to_all.64 = bf16[16,2,31616]{2,0,1:T(8,128)(2,1)S(1)} all-to-all(bf16[16,2,31616]{2,0,1:T(8,128)(2,1)S(1)} %bitcast.43), channel_id=1, replica_groups=mesh['rec'=2,'space'=16] {'rec'}, dimensions={1} | all-to-all | bytes 4046848 | tf_op jit(solution)/shard_map/all_to_all | solution.py:48
  206.3 2.3 fusion.2
  208.7 45.1 %all-reduce.2 = f32[32,32]{1,0:T(8,128)S(1)} all-reduce(f32[32,32]{1,0:T(8,128)S(1)} %fusion.2), channel_id=2, replica_groups=mesh['rec'=2,'space'=16] {'rec','space'}, use_global_device_ids=true, to_apply=%region_0.1.clone | all-reduce | flops 1024 | bytes 8192
  (20 shorter events, 10.1 us)
Async XLA Ops:
  0.0 5.8 %copy-start = (bf16[120,120]{1,0:T(8,128)(2,1)S(1)}, bf16[120,120]{1,0:T(8,128)(2,1)}, u32[]{:S(2)}) copy-start(bf16[120,120]{1,0:T(8,128)(2,1)} %param.7) | copy-start | bytes 86404
  12.0 2.8 %copy-start.4 = (bf16[70,70]{1,0:T(8,128)(2,1)S(1)}, bf16[70,70]{1,0:T(8,128)(2,1)}, u32[]{:S(2)}) copy-start(bf16[70,70]{1,0:T(8,128)(2,1)} %param.6) | copy-start | bytes 29404
  17.0 3.6 %copy-start.3 = (bf16[120,120]{1,0:T(8,128)(2,1)S(1)}, bf16[120,120]{1,0:T(8,128)(2,1)}, u32[]{:S(2)}) copy-start(bf16[120,120]{1,0:T(8,128)(2,1)} %param.5) | copy-start | bytes 86404
  71.4 8.5 %copy-start.2 = (bf16[1,120,8400]{2,1,0:T(8,128)(2,1)S(1)}, bf16[1,120,8400]{2,1,0:T(8,128)(2,1)}, u32[]{:S(2)}) copy-start(bf16[1,120,8400]{2,1,0:T(8,128)(2,1)} %param.4) | copy-start | bytes 6048004
  71.4 53.8 %all-to-all-start = ((bf16[16,2,31616]{2,1,0:T(2,128)(2,1)}), bf16[16,2,31616]{2,1,0:T(2,128)(2,1)}, u32[]{:S(2)}, u32[]{:S(2)}) async-start(bf16[16,2,31616]{2,1,0:T(2,128)(2,1)} %reshape.53), calls=%async_computation | async-start | bytes 4046848 | tf_op jit(solution)/shard_map/all_to_all | solution.py:42
  125.2 48.4 %all-to-all-start.2 = ((bf16[16,2,31616]{2,1,0:T(2,128)(2,1)}), bf16[16,2,31616]{2,1,0:T(2,128)(2,1)S(1)}, u32[]{:S(2)}, u32[]{:S(2)}) async-start(bf16[16,2,31616]{2,1,0:T(2,128)(2,1)} %reshape.55), calls=%async_computation.2 | async-start | bytes 4046848 | tf_op jit(solution)/shard_map/all_to_all | solution.py:49
  173.6 27.4 %all-to-all-start.1 = ((bf16[16,2,31616]{2,0,1:T(8,128)(2,1)}), bf16[16,2,31616]{2,0,1:T(8,128)(2,1)}, u32[]{:S(2)}, u32[]{:S(2)}) async-start(bf16[16,2,31616]{2,0,1:T(8,128)(2,1)} %bitcast.42), calls=%async_computation.1 | async-start | bytes 4046848 | tf_op jit(solution)/shard_map/all_to_all | solution.py:41
  206.3 47.9 %copy-start.1 = (bf16[120,120]{1,0:T(8,128)(2,1)S(1)}, bf16[120,120]{1,0:T(8,128)(2,1)}, u32[]{:S(2)}) copy-start(bf16[120,120]{1,0:T(8,128)(2,1)} %param.7) | copy-start | bytes 86404
where the time goes:
time: 255 us; the launch traced here: 254 us
  local copies, waits for them, and re-layouts  134 us (53%)
  blocking collectives  50.4 us (20%)
  other arithmetic  25.6 us (10%)
  starting transfers between devices  20.4 us (8%)
  waiting for transfers between devices  14.5 us (6%)
  matrix products  8.68 us (3%)
    unnamed x1, blocking collectives  45.1 us
    reshape x2, local copies, waits for them, and re-layouts, flatten_padded(): flat = values.reshape(receptors_here, -1)  43.2 us
    unnamed x18, local copies, waits for them, and re-layouts  35.3 us
    unnamed x2, other arithmetic  25.6 us
    all_to_all x1, waiting for transfers between devices, regroup(): lax.all_to_all(values[1], 'space', split_axis=1, concat_axis=0, tiled=True)  14.5 us
    all_to_all x1, local copies, waits for them, and re-layouts, regroup(): lax.all_to_all(values[0], 'space', split_axis=1, concat_axis=0, tiled=True)  13.2 us
    all_to_all x1, local copies, waits for them, and re-layouts, regroup(): lax.all_to_all(values[1], 'space', split_axis=1, concat_axis=0, tiled=True)  13.2 us
    pad x2, local copies, waits for them, and re-layouts, flatten_padded(): return jnp.pad(flat, ((0, 0), (0, per_device * devices - length)))  11.7 us
  transfers between devices with their start and end apart: 3, of which 1 were waited for; matrix products, arithmetic and copies ran while one was open for 37% of the time, Pallas kernels for 0%

commit v1 on v0

--- a/solution.py
+++ b/solution.py
@@ -2,6 +2,14 @@
 import jax.numpy as jnp
 from jax import lax
 from jax.sharding import PartitionSpec as P
+from jax.lax import all_to_all, axis_size
+
+
+def node_map(page, mesh_ax, d_out, along_dim):
+    f_now = all_to_all(
+        jnp.stack(jnp.split(page, axis_size(mesh_ax), axis=d_out), axis=0), mesh_ax, 0, 0
+    )
+    return jnp.concatenate(f_now, axis=along_dim)
 
 
 def weigh_footprints(footprints, time_cov, lat_cov, lon_cov):
@@ -39,11 +47,7 @@
 def regroup(values):
     moved = (
         lax.all_to_all(
-            lax.all_to_all(values[0], "space", split_axis=1, concat_axis=0, tiled=True),
-            "rec",
-            split_axis=1,
-            concat_axis=0,
-            tiled=True,
+            node_map(values[0], "space", 1, 0), "rec", split_axis=1, concat_axis=0, tiled=True
         ),
         lax.all_to_all(
             lax.all_to_all(values[1], "space", split_axis=1, concat_axis=0, tiled=True),

time: 255 us -> 267 us (1.047)
  other arithmetic: 25.6 us -> 40.4 us
    unnamed x18 -> x32, local copies, waits for them, and re-layouts: 35.3 us -> 50.8 us
    another operation x0 -> x1, other arithmetic: none -> 14.1 us  [node_map(): jnp.stack(jnp.split(page, axis_size(mesh_ax), axis=d_out), axis=0)]
    all_to_all x0 -> x1, other arithmetic: none -> 13.5 us  [node_map(): all_to_all(jnp.stack(jnp.split(page, axis_size(mesh_ax), axis=d_out), axi...]
    unnamed x2 -> x1, other arithmetic: 25.6 us -> 12.8 us
    all_to_all x2 -> x1, local copies, waits for them, and re-layouts: 14.6 us -> 3.02 us  [regroup(): lax.all_to_all(node_map(values[0], 'space', 1, 0), 'rec', split_axis=1, c...]
    pad x2 -> x1, local copies, waits for them, and re-layouts: 11.7 us -> 5.86 us  [flatten_padded(): return jnp.pad(flat, ((0, 0), (0, per_device * devices - length)))]
  transfers between devices with their start and end apart: 3 -> 3, of which waited for: 1 -> 1; matrix products, arithmetic and copies ran while one was open for 37% -> 36% of each run, Pallas kernels for 0% -> 0%
where the time goes in v1:
time: 267 us; the launch traced here: 266 us
  local copies, waits for them, and re-layouts  134 us (50%)
  blocking collectives  50.4 us (19%)
  other arithmetic  40.4 us (15%)
  starting transfers between devices  20 us (7%)
  waiting for transfers between devices  12.7 us (5%)
  matrix products  8.67 us (3%)
    unnamed x32, local copies, waits for them, and re-layouts  50.8 us
    unnamed x1, blocking collectives  45 us
    reshape x2, local copies, waits for them, and re-layouts, flatten_padded(): flat = values.reshape(receptors_here, -1)  43.2 us
    another operation x1, other arithmetic, node_map(): jnp.stack(jnp.split(page, axis_size(mesh_ax), axis=d_out), axis=0)  14.1 us
    all_to_all x1, other arithmetic, node_map(): all_to_all(jnp.stack(jnp.split(page, axis_size(mesh_ax), axis=d_out), axi...  13.5 us
    all_to_all x1, local copies, waits for them, and re-layouts, regroup(): lax.all_to_all(values[1], 'space', split_axis=1, concat_axis=0, tiled=True)  13.2 us
    unnamed x1, other arithmetic  12.8 us
    all_to_all x1, waiting for transfers between devices, regroup(): lax.all_to_all(values[1], 'space', split_axis=1, concat_axis=0, tiled=True)  12.7 us
  transfers between devices with their start and end apart: 3, of which 1 were waited for; matrix products, arithmetic and copies ran while one was open for 36% of the time, Pallas kernels for 0%

profile of v1, /device:TPU:0, one launch (start us, length us, event | category | flops | bytes accessed | tf_op | source)
XLA Modules:
  0.0 266.3 jit_solution(7906830817790890155)
XLA Ops:
  0.0 5.8 %reshape.36 = bf16[8400,120]{1,0:T(8,128)(2,1)S(1)} reshape(bf16[1,120,8400]{2,1,0:T(8,128)(2,1)} %param.4) | data formatting | bytes 4032000 | tf_op jit(solution)/shard_map/reshape | solution.py:20
  7.9 4.1 %copy.16 = bf16[8400,120]{1,0:T(8,128)(2,1)} copy(bf16[8400,120]{0,1:T(8,128)(2,1)} %convolution_convert_fusion.1) | data formatting | bytes 4032000 | tf_op jit(solution)/shard_map/convert_element_type | solution.py:23
  12.0 2.8 %reshape.37 = bf16[120,70,120]{2,1,0:T(8,128)(2,1)S(1)} reshape(bf16[8400,120]{1,0:T(8,128)(2,1)} %copy.16) | data formatting | bytes 4032000 | tf_op jit(solution)/shard_map/reshape | solution.py:26
  17.0 3.6 %copy.18 = bf16[120,70,120]{0,2,1:T(8,128)(2,1)S(1)} copy(bf16[120,70,120]{2,1,0:T(8,128)(2,1)} %convert_bitcast_fusion) | data formatting | bytes 4032000 | tf_op jit(solution)/shard_map/convert_element_type | solution.py:29
  22.7 4.7 %reshape.44 = bf16[1008000]{0:T(1024)(128)(2,1)S(1)} reshape(bf16[120,8400]{1,0:T(8,128)(2,1)} %fusion) | data formatting | bytes 4032000
  27.4 23.2 %reshape.39 = bf16[1,1008000]{1,0:T(2,128)(2,1)S(1)} reshape(bf16[1008000]{0:T(1024)(128)(2,1)S(1)} %reshape.44) | data formatting | bytes 4032000 | tf_op jit(solution)/shard_map/reshape | solution.py:40
  66.5 14.1 %reduce.3 = bf16[16,63232]{1,0:T(8,128)(2,1)} reduce(bf16[16,1,63232]{2,1,0:T(2,128)(2,1)} %fusion.2, bf16[]{:T(256)} %broadcast.6), dimensions={1}, to_apply=%fusion.2.reduce_sub_computation | reduce | bytes 4046850 | tf_op jit(solution)/shard_map/stack | solution.py:10
  80.6 2.9 %reshape.48 = bf16[16,2,31616]{2,1,0:T(2,128)(2,1)} reshape(bf16[16,63232]{1,0:T(8,128)(2,1)} %reduce.3) | data formatting | bytes 4046848
  83.6 8.4 %all-to-all-start = ((bf16[16,2,31616]{2,1,0:T(2,128)(2,1)}), bf16[16,2,31616]{2,1,0:T(2,128)(2,1)}, u32[]{:S(2)}, u32[]{:S(2)}) async-start(bf16[16,2,31616]{2,1,0:T(2,128)(2,1)} %reshape.48), calls=%async_computation | async-start | bytes 4046848 | tf_op jit(solution)/shard_map/all_to_all | solution.py:9
  92.0 5.0 %reshape.46 = bf16[1008000]{0:T(1024)(128)(2,1)} reshape(bf16[1,120,8400]{2,1,0:T(8,128)(2,1)S(1)} %copy-done.2) | data formatting | bytes 4032000
  96.9 20.0 %reshape.40 = bf16[1,1008000]{1,0:T(2,128)(2,1)S(1)} reshape(bf16[1008000]{0:T(1024)(128)(2,1)} %reshape.46) | data formatting | bytes 4032000 | tf_op jit(solution)/shard_map/reshape | solution.py:40
  116.9 5.9 %pad.8 = bf16[1,1011712]{1,0:T(2,128)(2,1)} pad(bf16[1,1008000]{1,0:T(2,128)(2,1)S(1)} %reshape.40, bf16[]{:T(256)} %constant.2.clone.1), padding=0_0x0_3712 | pad | bytes 4039426 | tf_op jit(solution)/shard_map/jit(_pad)/pad | solution.py:44
  122.8 12.8 %reduce.4 = bf16[16,63232]{1,0:T(8,128)(2,1)S(1)} reduce(bf16[16,1,63232]{2,1,0:T(2,128)(2,1)} %bitcast.97, bf16[]{:T(256)} %broadcast.6), dimensions={1}, to_apply=%bitcast.85.reduce_sub_computation | reduce | bytes 4046850
  137.2 6.8 %all-to-all-start.2 = ((bf16[16,2,31616]{2,1,0:T(2,128)(2,1)}), bf16[16,2,31616]{2,1,0:T(2,128)(2,1)S(1)}, u32[]{:S(2)}, u32[]{:S(2)}) async-start(bf16[16,2,31616]{2,1,0:T(2,128)(2,1)} %reshape.50), calls=%async_computation.2 | async-start | bytes 4046848 | tf_op jit(solution)/shard_map/all_to_all | solution.py:53
  144.1 12.4 %reshape.49 = bf16[16,1,63232]{2,1,0:T(2,128)(2,1)} reshape(bf16[16,2,31616]{2,1,0:T(2,128)(2,1)} %all-to-all-done) | data formatting | bytes 4046848
  156.5 13.5 %reduce = bf16[16,63232]{1,0:T(8,128)(2,1)} reduce(bf16[16,1,63232]{2,1,0:T(2,128)(2,1)} %reshape.49, bf16[]{:T(256)} %constant.11), dimensions={1}, to_apply=%all_to_all.41.reduce_sub_computation | reduce | bytes 4046850 | tf_op jit(solution)/shard_map/all_to_all | solution.py:9
  169.9 3.0 %copy.28 = bf16[2,2,8,31616]{3,2,0,1:T(8,128)(2,1)} copy(bf16[2,2,8,31616]{3,2,1,0:T(8,128)(2,1)} %bitcast.99) | data formatting | bytes 4046848 | tf_op jit(solution)/shard_map/all_to_all | solution.py:49
  172.9 12.7 %all-to-all-done.2 = bf16[16,2,31616]{2,1,0:T(2,128)(2,1)S(1)} async-done(((bf16[16,2,31616]{2,1,0:T(2,128)(2,1)}), bf16[16,2,31616]{2,1,0:T(2,128)(2,1)S(1)}, u32[]{:S(2)}, u32[]{:S(2)}) %all-to-all-start.2) | async-done | bytes 2023456 | tf_op jit(solution)/shard_map/all_to_all | solution.py:53
  185.6 4.8 %all-to-all-start.1 = ((bf16[16,2,31616]{2,0,1:T(8,128)(2,1)}), bf16[16,2,31616]{2,0,1:T(8,128)(2,1)}, u32[]{:S(2)}, u32[]{:S(2)}) async-start(bf16[16,2,31616]{2,0,1:T(8,128)(2,1)} %bitcast.101), calls=%async_computation.1 | async-start | bytes 4046848 | tf_op jit(solution)/shard_map/all_to_all | solution.py:49
  190.4 9.3 %reshape.51 = bf16[16,1,63232]{2,1,0:T(2,128)(2,1)} reshape(bf16[16,2,31616]{2,1,0:T(2,128)(2,1)S(1)} %all-to-all-done.2) | data formatting | bytes 4046848
  199.7 13.2 %bitcast_reduce_fusion = bf16[16,63232]{1,0:T(8,128)(2,1)S(1)} fusion(bf16[16,1,63232]{2,1,0:T(2,128)(2,1)} %reshape.51), kind=kLoop, calls=%fused_computation.41 | loop fusion | bytes 4046848 | tf_op jit(solution)/shard_map/all_to_all | solution.py:53
  213.0 5.4 %all_to_all.56 = bf16[16,2,31616]{2,0,1:T(8,128)(2,1)S(1)} all-to-all(bf16[16,2,31616]{2,0,1:T(8,128)(2,1)S(1)} %bitcast.102), channel_id=1, replica_groups=mesh['rec'=2,'space'=16] {'rec'}, dimensions={1} | all-to-all | bytes 4046848 | tf_op jit(solution)/shard_map/all_to_all | solution.py:52
  218.4 2.3 fusion.19
  220.7 45.0 %all-reduce.2 = f32[32,32]{1,0:T(8,128)S(1)} all-reduce(f32[32,32]{1,0:T(8,128)S(1)} %fusion.19), channel_id=2, replica_groups=mesh['rec'=2,'space'=16] {'rec','space'}, use_global_device_ids=true, to_apply=%region_0.1.clone | all-reduce | flops 1024 | bytes 8192
  (35 shorter events, 24.6 us)
Async XLA Ops:
  0.0 5.8 %copy-start = (bf16[120,120]{1,0:T(8,128)(2,1)S(1)}, bf16[120,120]{1,0:T(8,128)(2,1)}, u32[]{:S(2)}) copy-start(bf16[120,120]{1,0:T(8,128)(2,1)} %param.7) | copy-start | bytes 86404
  7.9 6.9 %copy-start.4 = (bf16[70,70]{1,0:T(8,128)(2,1)S(1)}, bf16[70,70]{1,0:T(8,128)(2,1)}, u32[]{:S(2)}) copy-start(bf16[70,70]{1,0:T(8,128)(2,1)} %param.6) | copy-start | bytes 29404
  14.8 5.8 %copy-start.3 = (bf16[120,120]{1,0:T(8,128)(2,1)S(1)}, bf16[120,120]{1,0:T(8,128)(2,1)}, u32[]{:S(2)}) copy-start(bf16[120,120]{1,0:T(8,128)(2,1)} %param.5) | copy-start | bytes 86404
  80.6 11.3 %copy-start.2 = (bf16[1,120,8400]{2,1,0:T(8,128)(2,1)S(1)}, bf16[1,120,8400]{2,1,0:T(8,128)(2,1)}, u32[]{:S(2)}) copy-start(bf16[1,120,8400]{2,1,0:T(8,128)(2,1)} %param.4) | copy-start | bytes 6048004
  83.6 53.7 %all-to-all-start = ((bf16[16,2,31616]{2,1,0:T(2,128)(2,1)}), bf16[16,2,31616]{2,1,0:T(2,128)(2,1)}, u32[]{:S(2)}, u32[]{:S(2)}) async-start(bf16[16,2,31616]{2,1,0:T(2,128)(2,1)} %reshape.48), calls=%async_computation | async-start | bytes 4046848 | tf_op jit(solution)/shard_map/all_to_all | solution.py:9
  137.2 48.4 %all-to-all-start.2 = ((bf16[16,2,31616]{2,1,0:T(2,128)(2,1)}), bf16[16,2,31616]{2,1,0:T(2,128)(2,1)S(1)}, u32[]{:S(2)}, u32[]{:S(2)}) async-start(bf16[16,2,31616]{2,1,0:T(2,128)(2,1)} %reshape.50), calls=%async_computation.2 | async-start | bytes 4046848 | tf_op jit(solution)/shard_map/all_to_all | solution.py:53
  185.6 27.4 %all-to-all-start.1 = ((bf16[16,2,31616]{2,0,1:T(8,128)(2,1)}), bf16[16,2,31616]{2,0,1:T(8,128)(2,1)}, u32[]{:S(2)}, u32[]{:S(2)}) async-start(bf16[16,2,31616]{2,0,1:T(8,128)(2,1)} %bitcast.101), calls=%async_computation.1 | async-start | bytes 4046848 | tf_op jit(solution)/shard_map/all_to_all | solution.py:49
  213.0 53.3 %copy-start.1 = (bf16[120,120]{1,0:T(8,128)(2,1)S(1)}, bf16[120,120]{1,0:T(8,128)(2,1)}, u32[]{:S(2)}) copy-start(bf16[120,120]{1,0:T(8,128)(2,1)} %param.7) | copy-start | bytes 86404
